TPU v7x, 32 devices: a whole 2x2x4 slice. The times are simulated.
32 devices in a mesh: dp: 2 (over y), seq: 16 (over z, x, core).
Axes of the slice: x: 2, y: 2, z: 4, core: 2. Of those that a mesh axis runs over, the one named last changes fastest.
Arguments:
- inputs: bfloat16 [2, 256, 512, 512], P('dp', 'seq'), may hold values from -6 to 6
- gate_logits: bfloat16 [2, 256, 512, 512], P('dp', 'seq'), may hold values from -8 to 8
- kernel: bfloat16 [256, 512, 512], P(None, 'seq'), may hold values from -1.5 to 1.5
- cotangent: bfloat16 [2, 256, 512, 512], P('dp', 'seq'), may hold values from -6 to 6
- block_one: bfloat16 [256, 512, 512], P('seq'), may hold values from -0.25 to 0.25
- block_two: bfloat16 [512, 256, 256], P('seq'), may hold values from -0.375 to 0.375
Outputs:
- output: bfloat16 [2, 256, 512, 512], P('dp', 'seq')
- grad_inputs: bfloat16 [2, 256, 512, 512], P('dp', 'seq')
- grad_gate: bfloat16 [2, 256, 512, 512], P('dp', 'seq')
- grad_kernel: bfloat16 [256, 512, 512], P(None, 'seq', 'dp')
- grad_block_one: bfloat16 [256, 512, 512], P('seq', None, 'dp')
- grad_block_two: bfloat16 [512, 256, 256], P('seq', None, 'dp')
All inputs are finite; a program needn't handle non-finite values.
Results may differ from a plain program's by a relative error of at most 0.009.
Values may be sent and summed in bfloat16 or wider, within the bound.
No kernel may reach another device: no remote copies, remote signals or barrier semaphores. Data moves between devices by JAX's collectives and lax.ppermute only.
A program may use at most 320 MiB of HBM per device.

v0:
```python
import jax
import jax.numpy as jnp
from jax import lax
from jax.sharding import PartitionSpec as P


def to_cols(x):
    return lax.all_to_all(x, "seq", split_axis=1, concat_axis=0, tiled=True)


def to_rows(x):
    return lax.all_to_all(x, "seq", split_axis=0, concat_axis=1, tiled=True)


def held(x):
    return lax.optimization_barrier(x)


def body(inputs, gate_logits, kernel, cotangent, block_one, block_two):
    tokens = inputs[0]
    kernel_wide = kernel.astype(jnp.float32)
    grad_scale = (lax.axis_size("dp") * tokens.shape[2]) ** (-0.5)
    f32 = jnp.float32
    opened = jax.nn.sigmoid(gate_logits[0].astype(f32))
    incoming = cotangent[0].astype(f32)
    grad_fourth = held((incoming * opened).astype(jnp.bfloat16))
    grad_third = jnp.einsum(
        "fch,fhd->fcd", block_one, grad_fourth, preferred_element_type=f32
    ).astype(jnp.bfloat16)
    grad_third_cols = to_cols(held(grad_third))
    first = jnp.einsum("acb,abd->acd", block_one, tokens, preferred_element_type=f32).astype(
        jnp.bfloat16
    )
    first, grad_third_cols = held((first, grad_third_cols))
    first_cols = to_cols(first)
    grad_filtered = held(
        jnp.einsum("cef,fcd->ecd", block_two, grad_third_cols, preferred_element_type=f32)
    )
    grad_second = (kernel_wide * grad_filtered).astype(jnp.bfloat16)
    grad_first = jnp.einsum(
        "cea,ecd->acd", block_two, grad_second, preferred_element_type=f32
    ).astype(jnp.bfloat16)
    grad_first, first_cols = held((grad_first, first_cols))
    grad_first_rows = to_rows(grad_first)
    second = held(jnp.einsum("cea,acd->ecd", block_two, first_cols, preferred_element_type=f32))
    filtered = (kernel_wide * second).astype(jnp.bfloat16)
    third = jnp.einsum("cef,ecd->fcd", block_two, filtered, preferred_element_type=f32).astype(
        jnp.bfloat16
    )
    third, grad_first_rows = held((third, grad_first_rows))
    third_rows = to_rows(third)
    grad_kernel = (grad_filtered * second).astype(jnp.bfloat16)
    grad_block_two = (
        (
            jnp.einsum("fcd,ecd->cef", grad_third_cols, filtered, preferred_element_type=f32)
            + jnp.einsum("ecd,acd->cea", grad_second, first_cols, preferred_element_type=f32)
        )
        * grad_scale
    ).astype(jnp.bfloat16)
    grad_kernel = lax.psum_scatter(grad_kernel, "dp", scatter_dimension=2, tiled=True)
    grad_block_two = lax.psum_scatter(grad_block_two, "dp", scatter_dimension=2, tiled=True)
    grad_tokens = jnp.einsum(
        "acb,acd->abd", block_one, grad_first_rows, preferred_element_type=f32
    ).astype(jnp.bfloat16)
    outer_inputs = jnp.einsum("acd,abd->acb", grad_first_rows, tokens, preferred_element_type=f32)
    fourth = jnp.einsum("fch,fcd->fhd", block_one, third_rows, preferred_element_type=f32).astype(
        jnp.bfloat16
    )
    fourth_wide = fourth.astype(f32)
    output = (opened * fourth_wide).astype(jnp.bfloat16)
    grad_gate = (incoming * fourth_wide * opened * (1.0 - opened)).astype(jnp.bfloat16)
    outer_one = jnp.einsum("fhd,fcd->fch", grad_fourth, third_rows, preferred_element_type=f32)
    grad_block_one = ((outer_one + outer_inputs) * grad_scale).astype(jnp.bfloat16)
    grad_block_one = lax.psum_scatter(grad_block_one, "dp", scatter_dimension=2, tiled=True)
    return (
        output[None],
        grad_tokens[None],
        grad_gate[None],
        grad_kernel,
        grad_block_one,
        grad_block_two,
    )


def solution(mesh):
    return jax.shard_map(
        body,
        mesh=mesh,
        in_specs=(
            P("dp", "seq", None, None),
            P("dp", "seq", None, None),
            P(None, "seq", None),
            P("dp", "seq", None, None),
            P("seq", None, None),
            P("seq", None, None),
        ),
        out_specs=(
            P("dp", "seq", None, None),
            P("dp", "seq", None, None),
            P("dp", "seq", None, None),
            P(None, "seq", "dp"),
            P("seq", None, "dp"),
            P("seq", None, "dp"),
        ),
        check_vma=False,
    )
```

profile of v0, /device:TPU:0, one launch (start us, length us, event | category | flops | bytes accessed | tf_op | source)
XLA Modules:
  0.0 1020.6 jit_solution(17853031852421777675)
XLA Ops:
  7.2 12.3 %copy.71 = bf16[1,16,512,512]{2,3,1,0:T(8,128)(2,1)} copy(bf16[1,16,512,512]{3,2,1,0:T(8,128)(2,1)} %param.7) | data formatting | bytes 16777216 | tf_op args[1]
  19.4 12.3 %copy.73 = bf16[1,16,512,512]{2,3,1,0:T(8,128)(2,1)} copy(bf16[1,16,512,512]{3,2,1,0:T(8,128)(2,1)} %param.9) | data formatting | bytes 16777216 | tf_op args[3]
  31.7 11.4 %fusion.2 = bf16[16,512,512]{1,2,0:T(8,128)(2,1)} fusion(bf16[1,16,512,512]{2,3,1,0:T(8,128)(2,1)} %copy.73, bf16[1,16,512,512]{2,3,1,0:T(8,128)(2,1)} %copy.71), kind=kLoop, calls=%fused_computation.6 | loop fusion | flops 29360128 | bytes 25165824 | tf_op jit(solution)/shard_map/convert_element_type | solution.py:26
  43.1 11.5 %convert_bitcast_fusion.3 = bf16[16,512,512]{1,2,0:T(8,128)(2,1)} fusion(bf16[16,512,512]{1,2,0:T(8,128)(2,1)} %fusion.2, bf16[16,512,512]{2,1,0:T(8,128)(2,1)} %param.10), kind=kOutput, calls=%fused_computation.28 | convolution fusion | flops 4299161600 | bytes 25165824 | tf_op jit(solution)/shard_map/fch,fhd->fcd/dot_general | solution.py:27
  54.5 14.9 %copy.74 = bf16[16,512,512]{2,0,1:T(8,128)(2,1)} copy(bf16[16,512,512]{1,2,0:T(8,128)(2,1)} %convert_bitcast_fusion.3) | data formatting | bytes 16777216 | tf_op jit(solution)/shard_map/optimization_barrier | solution.py:16
  69.4 7.9 all-to-all-start
  77.3 13.7 %fusion.16 = bf16[16,512,512]{2,1,0:T(8,128)(2,1)} fusion(bf16[16,512,512]{2,1,0:T(8,128)(2,1)} %param.10, bf16[1,16,512,512]{3,2,1,0:T(8,128)(2,1)} %param.6), kind=kOutput, calls=%fused_computation.32 | convolution fusion | flops 4299161600 | bytes 25165824 | tf_op jit(solution)/shard_map/acb,abd->acd/dot_general | solution.py:31
  91.0 136.4 %all-to-all-done = bf16[16,512,512]{2,0,1:T(8,128)(2,1)} async-done(((bf16[16,512,512]{2,0,1:T(8,128)(2,1)}), bf16[16,512,512]{2,0,1:T(8,128)(2,1)}, u32[]{:S(2)}, u32[]{:S(2)}) %all-to-all-start) | async-done | bytes 8388640 | tf_op jit(solution)/shard_map/all_to_all | solution.py:8
  227.4 12.3 %copy.76 = bf16[16,16,32,512]{3,2,1,0:T(8,128)(2,1)} copy(bf16[16,16,32,512]{3,1,2,0:T(8,128)(2,1)} %bitcast.6) | data formatting | bytes 16777216 | tf_op jit(solution)/shard_map/all_to_all | solution.py:8
  239.7 11.5 %copy.78 = bf16[16,512,512]{2,0,1:T(8,128)(2,1)} copy(bf16[16,512,512]{2,1,0:T(8,128)(2,1)} %fusion.16) | data formatting | bytes 16777216 | tf_op jit(solution)/shard_map/optimization_barrier | solution.py:16
  251.3 36.5 %all-to-all-start.1 = ((bf16[16,512,512]{2,0,1:T(8,128)(2,1)}), bf16[16,512,512]{2,0,1:T(8,128)(2,1)}, u32[]{:S(2)}, u32[]{:S(2)}) async-start(bf16[16,512,512]{2,0,1:T(8,128)(2,1)} %copy.78), calls=%async_computation.1 | async-start | bytes 16777216 | tf_op jit(solution)/shard_map/all_to_all | solution.py:8
  287.8 13.7 %copy.72 = bf16[256,32,512]{0,2,1:T(8,128)(2,1)} copy(bf16[256,32,512]{2,1,0:T(8,128)(2,1)} %param.8) | data formatting | bytes 16777216 | tf_op args[2]
  301.5 20.4 %convolution_bitcast_fusion.1 = f32[256,32,512]{0,2,1:T(8,128)} fusion(bf16[32,256,256]{2,1,0:T(8,128)(2,1)} %param.11, bf16[256,32,512]{2,1,0:T(8,128)(2,1)} %bitcast.90), kind=kOutput, calls=%fused_computation.17 | convolution fusion | flops 2147483648 | bytes 29360128 | tf_op jit(solution)/shard_map/cef,fcd->ecd/dot_general | solution.py:37
  321.9 14.5 %convert_bitcast_fusion.2 = bf16[256,32,512]{0,2,1:T(8,128)(2,1)} fusion(bf16[32,256,256]{2,1,0:T(8,128)(2,1)} %param.11, f32[256,32,512]{0,2,1:T(8,128)} %convolution_bitcast_fusion.1, bf16[256,32,512]{0,2,1:T(8,128)(2,1)} %copy.72), kind=kOutput, calls=%fused_computation.27 | convolution fusion | flops 2164260864 | bytes 37748736 | tf_op jit(solution)/shard_map/cea,ecd->acd/dot_general | solution.py:40
  336.4 102.0 %all-to-all-done.1 = bf16[16,512,512]{2,0,1:T(8,128)(2,1)} async-done(((bf16[16,512,512]{2,0,1:T(8,128)(2,1)}), bf16[16,512,512]{2,0,1:T(8,128)(2,1)}, u32[]{:S(2)}, u32[]{:S(2)}) %all-to-all-start.1) | async-done | bytes 8388640 | tf_op jit(solution)/shard_map/all_to_all | solution.py:8
  438.4 8.2 copy.79
  446.6 14.7 %copy.81 = bf16[256,32,512]{2,1,0:T(8,128)(2,1)} copy(bf16[256,32,512]{0,2,1:T(8,128)(2,1)} %convert_bitcast_fusion.2) | data formatting | bytes 16777216 | tf_op jit(solution)/shard_map/optimization_barrier | solution.py:16
  461.3 36.5 %all-to-all-start.2 = ((bf16[256,32,512]{2,1,0:T(8,128)(2,1)}), bf16[256,32,512]{2,1,0:T(8,128)(2,1)}, u32[]{:S(2)}, u32[]{:S(2)}) async-start(bf16[256,32,512]{2,1,0:T(8,128)(2,1)} %copy.81), calls=%async_computation.2 | async-start | bytes 16777216 | tf_op jit(solution)/shard_map/all_to_all | solution.py:12
  497.8 0.0 reduce-scatter.10.cloned.1.call-start
  497.9 12.8 %convolution_bitcast_fusion = f32[256,32,512]{0,2,1:T(8,128)} fusion(bf16[256,32,512]{2,0,1:T(8,128)(2,1)} %bitcast.88, bf16[32,256,256]{2,1,0:T(8,128)(2,1)} %param.11), kind=kOutput, calls=%fused_computation.16 | convolution fusion | flops 2147483648 | bytes 29360128 | tf_op jit(solution)/shard_map/cea,acd->ecd/dot_general | solution.py:45
  510.6 21.2 %fusion.14 = f32[32,256,256]{2,1,0:T(8,128)} fusion(bf16[256,32,512]{2,1,0:T(8,128)(2,1)} %bitcast.91, f32[256,32,512]{0,2,1:T(8,128)} %convolution_bitcast_fusion, bf16[256,32,512]{0,2,1:T(8,128)(2,1)} %copy.72), kind=kOutput, calls=%fused_computation.30 | convolution fusion | flops 2160066560 | bytes 41943040 | tf_op jit(solution)/shard_map/fcd,ecd->cef/dot_general | solution.py:55
  531.8 16.4 %multiply_convert_fusion.2 = bf16[32,256,256]{2,1,0:T(8,128)(2,1)} fusion(f32[32,256,256]{2,1,0:T(8,128)} %fusion.14, bf16[256,32,512]{2,0,1:T(8,128)(2,1)} %bitcast.89, f32[256,32,512]{0,2,1:T(8,128)} %convolution_bitcast_fusion.1, bf16[256,32,512]{0,2,1:T(8,128)(2,1)} %copy.72), kind=kOutput, calls=%fused_computation.24 | convolution fusion | flops 2166358016 | bytes 46137344 | tf_op jit(solution)/shard_map/ecd,acd->cea/dot_general | solution.py:56
  548.2 8.0 copy.102
  556.2 8.5 copy.104
  564.7 0.0 reduce-scatter.10.cloned.1.call-update
  564.7 14.6 %convert_bitcast_fusion.1 = bf16[256,32,512]{0,2,1:T(8,128)(2,1)} fusion(bf16[32,256,256]{2,1,0:T(8,128)(2,1)} %param.11, f32[256,32,512]{0,2,1:T(8,128)} %convolution_bitcast_fusion, bf16[256,32,512]{0,2,1:T(8,128)(2,1)} %copy.72), kind=kOutput, calls=%fused_computation.26 | convolution fusion | flops 2164260864 | bytes 37748736 | tf_op jit(solution)/shard_map/cef,ecd->fcd/dot_general | solution.py:47
  579.3 69.1 %all-to-all-done.2 = bf16[256,32,512]{2,1,0:T(8,128)(2,1)} async-done(((bf16[256,32,512]{2,1,0:T(8,128)(2,1)}), bf16[256,32,512]{2,1,0:T(8,128)(2,1)}, u32[]{:S(2)}, u32[]{:S(2)}) %all-to-all-start.2) | async-done | bytes 8388640 | tf_op jit(solution)/shard_map/all_to_all | solution.py:12
  648.4 8.3 copy.82
  656.7 14.7 %copy.83 = bf16[256,32,512]{2,1,0:T(8,128)(2,1)} copy(bf16[256,32,512]{0,2,1:T(8,128)(2,1)} %convert_bitcast_fusion.1) | data formatting | bytes 16777216 | tf_op jit(solution)/shard_map/optimization_barrier | solution.py:16
  671.3 36.5 %all-to-all-start.3 = ((bf16[256,32,512]{2,1,0:T(8,128)(2,1)}), bf16[256,32,512]{2,1,0:T(8,128)(2,1)}, u32[]{:S(2)}, u32[]{:S(2)}) async-start(bf16[256,32,512]{2,1,0:T(8,128)(2,1)} %copy.83), calls=%async_computation.3 | async-start | bytes 16777216 | tf_op jit(solution)/shard_map/all_to_all | solution.py:12
  707.9 0.0 reduce-scatter.6.cloned.1.call-start
  707.9 14.9 %multiply_convert_fusion.1 = bf16[256,32,512]{0,2,1:T(8,128)(2,1)} fusion(f32[256,32,512]{0,2,1:T(8,128)} %convolution_bitcast_fusion.1, f32[256,32,512]{0,2,1:T(8,128)} %convolution_bitcast_fusion), kind=kLoop, calls=%fused_computation.14 | loop fusion | flops 8388608 | bytes 41943040 | tf_op jit(solution)/shard_map/convert_element_type | solution.py:52
  722.9 0.0 reduce-scatter.6.cloned.1.call-update
  722.9 0.0 reduce-scatter.8.cloned.1.call-start
  722.9 16.1 %fusion.9 = f32[16,512,512]{2,1,0:T(8,128)} fusion(bf16[16,512,512]{2,1,0:T(8,128)(2,1)} %bitcast.92, bf16[1,16,512,512]{3,2,1,0:T(8,128)(2,1)} %param.6), kind=kOutput, calls=%fused_computation.20 | convolution fusion | flops 4294967296 | bytes 33554432 | tf_op jit(solution)/shard_map/acd,abd->acb/dot_general | solution.py:65
  739.0 119.5 %all-to-all-done.3 = bf16[256,32,512]{2,1,0:T(8,128)(2,1)} async-done(((bf16[256,32,512]{2,1,0:T(8,128)(2,1)}), bf16[256,32,512]{2,1,0:T(8,128)(2,1)}, u32[]{:S(2)}, u32[]{:S(2)}) %all-to-all-start.3) | async-done | bytes 8388640 | tf_op jit(solution)/shard_map/all_to_all | solution.py:12
  858.5 8.3 copy.84
  866.7 15.7 %multiply_convert_fusion = bf16[16,512,512]{2,1,0:T(8,128)(2,1)} fusion(f32[16,512,512]{2,1,0:T(8,128)} %fusion.9, bf16[16,512,512]{2,1,0:T(8,128)(2,1)} %bitcast.94, bf16[16,512,512]{1,2,0:T(8,128)(2,1)} %fusion.2), kind=kOutput, calls=%fused_computation.13 | convolution fusion | flops 4307550208 | bytes 41943040 | tf_op jit(solution)/shard_map/fhd,fcd->fch/dot_general | solution.py:72
  882.4 0.0 reduce-scatter.8.cloned.1.call-update
  882.5 0.0 reduce-scatter.10.cloned.1.call-done
  882.5 2.2 copy.105
  884.7 3.0 copy.103
  887.7 11.4 %convert_bitcast_fusion = bf16[1,16,512,512]{2,3,1,0:T(8,128)(2,1)} fusion(bf16[16,512,512]{2,1,0:T(8,128)(2,1)} %bitcast.93, bf16[16,512,512]{2,1,0:T(8,128)(2,1)} %param.10), kind=kOutput, calls=%fused_computation.25 | convolution fusion | flops 4299161600 | bytes 25165824 | tf_op jit(solution)/shard_map/acb,acd->abd/dot_general | solution.py:62
  899.1 12.3 %copy.92 = bf16[1,16,512,512]{3,2,1,0:T(8,128)(2,1)} copy(bf16[1,16,512,512]{2,3,1,0:T(8,128)(2,1)} %convert_bitcast_fusion) | data formatting | bytes 16777216
  911.4 0.0 reduce-scatter.6.cloned.1.call-done
  911.4 7.8 copy.94
  919.2 21.2 %fusion.8 = (bf16[1,16,512,512]{2,3,1,0:T(8,128)(2,1)}, bf16[1,16,512,512]{2,3,1,0:T(8,128)(2,1)}) fusion(bf16[1,16,512,512]{2,3,1,0:T(8,128)(2,1)} %copy.73, bf16[1,16,512,512]{2,3,1,0:T(8,128)(2,1)} %copy.71, bf16[16,512,512]{2,1,0:T(8,128)(2,1)} %bitcast.95, bf16[16,512,512]{2,1,0:T(8,128)(2,1)} %param.10), kind=kOutput, calls=%fused_computation.19 | convolution fusion | flops 4353687552 | bytes 50331648 | tf_op jit(solution)/shard_map/fch,fcd->fhd/dot_general | solution.py:66
  940.4 12.4 %copy.93 = bf16[1,16,512,512]{3,2,1,0:T(8,128)(2,1)} copy(bf16[1,16,512,512]{2,3,1,0:T(8,128)(2,1)} %get-tuple-element.42) | data formatting | bytes 16777216
  952.8 12.3 %copy.91 = bf16[1,16,512,512]{3,2,1,0:T(8,128)(2,1)} copy(bf16[1,16,512,512]{2,3,1,0:T(8,128)(2,1)} %get-tuple-element.43) | data formatting | bytes 16777216
  965.1 48.7 %reduce-scatter.8.cloned.1.call-done = bf16[16,512,256]{2,1,0:T(8,128)(2,1)} async-done(((bf16[16,512,512]{2,1,0:T(8,128)(2,1)}), bf16[16,512,256]{2,1,0:T(8,128)(2,1)}) %reduce-scatter.8.cloned.1.call-update) | async-done | bytes 4194320 | tf_op jit(solution)/shard_map/reduce_scatter | solution.py:74
Async XLA Ops:
  69.4 158.0 %all-to-all-start = ((bf16[16,512,512]{2,0,1:T(8,128)(2,1)}), bf16[16,512,512]{2,0,1:T(8,128)(2,1)}, u32[]{:S(2)}, u32[]{:S(2)}) async-start(bf16[16,512,512]{2,0,1:T(8,128)(2,1)} %copy.74), calls=%async_computation | async-start | bytes 16777216 | tf_op jit(solution)/shard_map/all_to_all | solution.py:8
  251.3 187.1 %all-to-all-start.1 = ((bf16[16,512,512]{2,0,1:T(8,128)(2,1)}), bf16[16,512,512]{2,0,1:T(8,128)(2,1)}, u32[]{:S(2)}, u32[]{:S(2)}) async-start(bf16[16,512,512]{2,0,1:T(8,128)(2,1)} %copy.78), calls=%async_computation.1 | async-start | bytes 16777216 | tf_op jit(solution)/shard_map/all_to_all | solution.py:8
  461.3 187.1 %all-to-all-start.2 = ((bf16[256,32,512]{2,1,0:T(8,128)(2,1)}), bf16[256,32,512]{2,1,0:T(8,128)(2,1)}, u32[]{:S(2)}, u32[]{:S(2)}) async-start(bf16[256,32,512]{2,1,0:T(8,128)(2,1)} %copy.81), calls=%async_computation.2 | async-start | bytes 16777216 | tf_op jit(solution)/shard_map/all_to_all | solution.py:12
  497.8 384.7 %reduce-scatter.10.cloned.1.call-start = ((), (), s32[]{:S(2)}) async-start(), calls=%async_computation.9 | async-start | bytes 6291456
  671.3 187.1 %all-to-all-start.3 = ((bf16[256,32,512]{2,1,0:T(8,128)(2,1)}), bf16[256,32,512]{2,1,0:T(8,128)(2,1)}, u32[]{:S(2)}, u32[]{:S(2)}) async-start(bf16[256,32,512]{2,1,0:T(8,128)(2,1)} %copy.83), calls=%async_computation.3 | async-start | bytes 16777216 | tf_op jit(solution)/shard_map/all_to_all | solution.py:12
  707.9 203.5 %reduce-scatter.6.cloned.1.call-start = ((), (), s32[]{:S(2)}) async-start(), calls=%async_computation.7 | async-start | bytes 12582912 | tf_op jit(solution)/shard_map/reduce_scatter | solution.py:60
  722.9 290.9 %reduce-scatter.8.cloned.1.call-start = ((), (), s32[]{:S(2)}) async-start(), calls=%async_computation.8 | async-start | bytes 12582912 | tf_op jit(solution)/shard_map/reduce_scatter | solution.py:74
Sparse Core Ops, SparseCore 0:
  564.9 55.6 reduce-scatter.9
  723.0 100.6 reduce-scatter.5
  882.6 131.1 reduce-scatter.7
where the time goes:
time: 1030 us; the launch traced here: 1020 us
  waiting for transfers between devices  476 us (46%)
  local copies, waits for them, and re-layouts  198 us (19%)
  matrix products  189 us (18%)
  starting transfers between devices  118 us (11%)
  other arithmetic  26.3 us (3%)
  between operations  14 us (1%)
    all_to_all x2, waiting for transfers between devices, to_cols(): return lax.all_to_all(x, 'seq', split_axis=1, concat_axis=0, tiled=True)  238 us
    all_to_all x2, waiting for transfers between devices, to_rows(): return lax.all_to_all(x, 'seq', split_axis=0, concat_axis=1, tiled=True)  189 us
    unnamed x11, local copies, waits for them, and re-layouts  105 us
    all_to_all x2, starting transfers between devices, to_rows(): return lax.all_to_all(x, 'seq', split_axis=0, concat_axis=1, tiled=True)  73.1 us
    optimization_barrier x4, local copies, waits for them, and re-layouts, held(): return lax.optimization_barrier(x)  55.8 us
    reduce_scatter x1, waiting for transfers between devices, body(): lax.psum_scatter(grad_block_one, 'dp', scatter_dimension=2, tiled=True)  48.7 us
    all_to_all x2, starting transfers between devices, to_cols(): return lax.all_to_all(x, 'seq', split_axis=1, concat_axis=0, tiled=True)  44.4 us
    dot_general x1, matrix products, body(): jnp.einsum('fch,fcd->fhd', block_one, third_rows, preferred_element_type=...  21.2 us
  transfers between devices with their start and end apart: 7, of which 5 were waited for; matrix products, arithmetic and copies ran while one was open for 30% of the time, Pallas kernels for 0%

commit v1 on v0

--- a/solution.py
+++ b/solution.py
@@ -5,7 +5,9 @@
 
 
 def to_cols(x):
-    return lax.all_to_all(x, "seq", split_axis=1, concat_axis=0, tiled=True)
+    return jnp.concatenate(
+        lax.all_to_all(jnp.stack(jnp.split(x, lax.axis_size("seq"), axis=1)), "seq", 0, 0), axis=0
+    )
 
 
 def to_rows(x):

time: 1030 us -> 1090 us (1.058)
  local copies, waits for them, and re-layouts: 198 us -> 256 us
  matrix products: 189 us -> 203 us
  waiting for transfers between devices: 476 us -> 463 us
    another operation x0 -> x19, local copies, waits for them, and re-layouts: none -> 62.5 us  [to_cols(): jnp.stack(jnp.split(x, lax.axis_size('seq'), axis=1))]
    unnamed x11 -> x55, local copies, waits for them, and re-layouts: 105 us -> 148 us
    optimization_barrier x4 -> x2, local copies, waits for them, and re-layouts: 55.8 us -> 29.2 us  [held(): return lax.optimization_barrier(x)]
    all_to_all x2 -> x0, local copies, waits for them, and re-layouts: 20.5 us -> none  [to_cols(): return lax.all_to_all(x, 'seq', split_axis=1, concat_axis=0, tiled=True)]
    all_to_all x2, waiting for transfers between devices: 189 us -> 175 us  [to_rows(): return lax.all_to_all(x, 'seq', split_axis=0, concat_axis=1, tiled=True)]
  transfers between devices with their start and end apart: 7 -> 7, of which waited for: 5 -> 5; matrix products, arithmetic and copies ran while one was open for 30% -> 29% of each run, Pallas kernels for 0% -> 0%
where the time goes in v1:
time: 1090 us; the launch traced here: 1080 us
  waiting for transfers between devices  463 us (42%)
  local copies, waits for them, and re-layouts  256 us (23%)
  matrix products  203 us (19%)
  starting transfers between devices  117 us (11%)
  other arithmetic  26.3 us (2%)
  between operations  14.3 us (1%)
    all_to_all x2, waiting for transfers between devices, to_cols(): lax.all_to_all(jnp.stack(jnp.split(x, lax.axis_size('seq'), axis=1)), 'se...  239 us
    all_to_all x2, waiting for transfers between devices, to_rows(): return lax.all_to_all(x, 'seq', split_axis=0, concat_axis=1, tiled=True)  175 us
    unnamed x55, local copies, waits for them, and re-layouts  148 us
    all_to_all x2, starting transfers between devices, to_rows(): return lax.all_to_all(x, 'seq', split_axis=0, concat_axis=1, tiled=True)  73.1 us
    another operation x19, local copies, waits for them, and re-layouts, to_cols(): jnp.stack(jnp.split(x, lax.axis_size('seq'), axis=1))  62.5 us
    reduce_scatter x1, waiting for transfers between devices, body(): lax.psum_scatter(grad_block_one, 'dp', scatter_dimension=2, tiled=True)  48.7 us
    all_to_all x2, starting transfers between devices, to_cols(): lax.all_to_all(jnp.stack(jnp.split(x, lax.axis_size('seq'), axis=1)), 'se...  44.2 us
    optimization_barrier x2, local copies, waits for them, and re-layouts, held(): return lax.optimization_barrier(x)  29.2 us
  transfers between devices with their start and end apart: 7, of which 5 were waited for; matrix products, arithmetic and copies ran while one was open for 29% of the time, Pallas kernels for 0%

profile of v1, /device:TPU:0, one launch (start us, length us, event | category | flops | bytes accessed | tf_op | source)
XLA Modules:
  0.0 1079.6 jit_solution(10921028470349587351)
XLA Ops:
  7.2 12.3 %copy.69 = bf16[1,16,512,512]{2,3,1,0:T(8,128)(2,1)} copy(bf16[1,16,512,512]{3,2,1,0:T(8,128)(2,1)} %param.7) | data formatting | bytes 16777216 | tf_op args[1]
  19.4 12.3 %copy.71 = bf16[1,16,512,512]{2,3,1,0:T(8,128)(2,1)} copy(bf16[1,16,512,512]{3,2,1,0:T(8,128)(2,1)} %param.9) | data formatting | bytes 16777216 | tf_op args[3]
  31.7 11.4 %fusion.2 = bf16[16,512,512]{1,2,0:T(8,128)(2,1)} fusion(bf16[1,16,512,512]{2,3,1,0:T(8,128)(2,1)} %copy.71, bf16[1,16,512,512]{2,3,1,0:T(8,128)(2,1)} %copy.69), kind=kLoop, calls=%fused_computation.6 | loop fusion | flops 29360128 | bytes 25165824 | tf_op jit(solution)/shard_map/convert_element_type | solution.py:28
  43.1 11.5 %convert_bitcast_fusion.3 = bf16[16,512,512]{1,2,0:T(8,128)(2,1)} fusion(bf16[16,512,512]{1,2,0:T(8,128)(2,1)} %fusion.2, bf16[16,512,512]{2,1,0:T(8,128)(2,1)} %param.10), kind=kOutput, calls=%fused_computation.28 | convolution fusion | flops 4299161600 | bytes 25165824 | tf_op jit(solution)/shard_map/fch,fhd->fcd/dot_general | solution.py:29
  54.5 22.1 %slice_bitcast_fusion = (bf16[1,16,32,512]{2,3,1,0:T(8,128)(2,1)}, bf16[1,16,32,512]{2,3,1,0:T(8,128)(2,1)}, bf16[1,16,32,512]{2,3,1,0:T(8,128)(2,1)}, bf16[1,16...) fusion(bf16[16,512,512]{1,2,0:T(8,128)(2,1)} %convert_bitcast_f, ...), kind=kLoop, calls=%fused_computation.37 | loop fusion | bytes 16777216 | tf_op jit(solution)/shard_map/stack | solution.py:9
  80.4 2.6 copy.85
  83.0 2.6 copy.84
  85.5 2.6 copy.83
  88.1 2.6 copy.82
  90.7 2.6 copy.81
  93.2 2.6 copy.80
  95.8 2.6 copy.79
  98.4 2.6 copy.78
  101.0 2.6 copy.77
  103.6 2.6 copy.76
  106.2 2.6 copy.75
  108.7 2.6 copy.74
  111.3 2.6 copy.73
  115.4 2.0 constant_dynamic-update-slice_fusion.15
  117.4 1.9 constant_dynamic-update-slice_fusion.14
  119.3 1.9 constant_dynamic-update-slice_fusion.13
  121.2 1.9 constant_dynamic-update-slice_fusion.12
  123.1 1.9 constant_dynamic-update-slice_fusion.11
  125.0 1.9 constant_dynamic-update-slice_fusion.10
  128.8 1.9 constant_dynamic-update-slice_fusion.8
  137.5 7.6 all-to-all-start
  145.1 13.7 %fusion.19 = bf16[16,512,512]{2,1,0:T(8,128)(2,1)} fusion(bf16[16,512,512]{2,1,0:T(8,128)(2,1)} %param.10, bf16[1,16,512,512]{3,2,1,0:T(8,128)(2,1)} %param.6), kind=kOutput, calls=%fused_computation.35 | convolution fusion | flops 4299161600 | bytes 25165824 | tf_op jit(solution)/shard_map/acb,abd->acd/dot_general | solution.py:33
  158.8 136.9 %all-to-all-done = bf16[16,16,32,512]{3,2,1,0:T(8,128)(2,1)} async-done(((bf16[16,16,32,512]{3,2,1,0:T(8,128)(2,1)}), bf16[16,16,32,512]{3,2,1,0:T(8,128)(2,1)}, u32[]{:S(2)}, u32[]{:S(2)}) %all-to-all-start) | async-done | bytes 8388640 | tf_op jit(solution)/shard_map/all_to_all | solution.py:9
  295.7 2.0 bitcast_dynamic-update-slice_fusion.15
  297.7 2.6 bitcast_dynamic-update-slice_fusion.14
  300.3 1.9 bitcast_dynamic-update-slice_fusion.13
  302.2 1.9 bitcast_dynamic-update-slice_fusion.12
  307.9 1.9 bitcast_dynamic-update-slice_fusion.9
  318.5 36.5 %all-to-all-start.1 = ((bf16[16,16,32,512]{3,2,1,0:T(8,128)(2,1)}), bf16[16,16,32,512]{3,2,1,0:T(8,128)(2,1)}, u32[]{:S(2)}, u32[]{:S(2)}) async-start(bf16[16,16,32,512]{3,2,1,0:T(8,128)(2,1)} %bitcast_dynamic-update-slice_fusion), calls=%async_computation.1 | async-start | bytes 16777216 | tf_op jit(solution)/shard_map/all_to_all | solution.py:9
  355.0 13.7 %copy.70 = bf16[256,32,512]{0,2,1:T(8,128)(2,1)} copy(bf16[256,32,512]{2,1,0:T(8,128)(2,1)} %param.8) | data formatting | bytes 16777216 | tf_op args[2]
  368.7 20.4 %convolution_bitcast_fusion.1 = f32[256,32,512]{0,2,1:T(8,128)} fusion(bf16[32,256,256]{2,1,0:T(8,128)(2,1)} %param.11, bf16[256,32,512]{2,1,0:T(8,128)(2,1)} %bitcast.20), kind=kOutput, calls=%fused_computation.17 | convolution fusion | flops 2147483648 | bytes 29360128 | tf_op jit(solution)/shard_map/cef,fcd->ecd/dot_general | solution.py:39
  389.1 14.5 %convert_bitcast_fusion.2 = bf16[256,32,512]{0,2,1:T(8,128)(2,1)} fusion(bf16[32,256,256]{2,1,0:T(8,128)(2,1)} %param.11, f32[256,32,512]{0,2,1:T(8,128)} %convolution_bitcast_fusion.1, bf16[256,32,512]{0,2,1:T(8,128)(2,1)} %copy.70), kind=kOutput, calls=%fused_computation.27 | convolution fusion | flops 2164260864 | bytes 37748736 | tf_op jit(solution)/shard_map/cea,ecd->acd/dot_general | solution.py:42
  403.6 102.0 %all-to-all-done.1 = bf16[16,16,32,512]{3,2,1,0:T(8,128)(2,1)} async-done(((bf16[16,16,32,512]{3,2,1,0:T(8,128)(2,1)}), bf16[16,16,32,512]{3,2,1,0:T(8,128)(2,1)}, u32[]{:S(2)}, u32[]{:S(2)}) %all-to-all-start.1) | async-done | bytes 8388640 | tf_op jit(solution)/shard_map/all_to_all | solution.py:9
  505.6 14.6 %copy.90 = bf16[256,32,512]{2,1,0:T(8,128)(2,1)} copy(bf16[256,32,512]{0,2,1:T(8,128)(2,1)} %convert_bitcast_fusion.2) | data formatting | bytes 16777216 | tf_op jit(solution)/shard_map/optimization_barrier | solution.py:18
  520.2 36.5 %all-to-all-start.2 = ((bf16[256,32,512]{2,1,0:T(8,128)(2,1)}), bf16[256,32,512]{2,1,0:T(8,128)(2,1)}, u32[]{:S(2)}, u32[]{:S(2)}) async-start(bf16[256,32,512]{2,1,0:T(8,128)(2,1)} %copy.90), calls=%async_computation.2 | async-start | bytes 16777216 | tf_op jit(solution)/shard_map/all_to_all | solution.py:14
  556.8 20.4 %convolution_bitcast_fusion = f32[256,32,512]{0,2,1:T(8,128)} fusion(bf16[32,256,256]{2,1,0:T(8,128)(2,1)} %param.11, bf16[256,32,512]{2,1,0:T(8,128)(2,1)} %bitcast.39), kind=kOutput, calls=%fused_computation.16 | convolution fusion | flops 2147483648 | bytes 29360128 | tf_op jit(solution)/shard_map/cea,acd->ecd/dot_general | solution.py:47
  577.2 21.3 %fusion.14 = f32[32,256,256]{2,1,0:T(8,128)} fusion(bf16[256,32,512]{2,1,0:T(8,128)(2,1)} %bitcast.39, f32[256,32,512]{0,2,1:T(8,128)} %convolution_bitcast_fusion.1, bf16[256,32,512]{0,2,1:T(8,128)(2,1)} %copy.70), kind=kOutput, calls=%fused_computation.30 | convolution fusion | flops 2160066560 | bytes 41943040 | tf_op jit(solution)/shard_map/ecd,acd->cea/dot_general | solution.py:58
  598.5 22.0 %multiply_convert_fusion.2 = bf16[32,256,256]{2,1,0:T(8,128)(2,1)} fusion(f32[32,256,256]{2,1,0:T(8,128)} %fusion.14, bf16[256,32,512]{2,1,0:T(8,128)(2,1)} %bitcast.20, f32[256,32,512]{0,2,1:T(8,128)} %convolution_bitcast_fusion, bf16[256,32,512]{0,2,1:T(8,128)(2,1)} %copy.70), kind=kOutput, calls=%fused_computation.24 | convolution fusion | flops 2166358016 | bytes 46137344 | tf_op jit(solution)/shard_map/fcd,ecd->cef/dot_general | solution.py:57
  620.6 8.0 copy.110
  628.6 8.5 copy.112
  637.1 14.5 %convert_bitcast_fusion.1 = bf16[256,32,512]{0,2,1:T(8,128)(2,1)} fusion(bf16[32,256,256]{2,1,0:T(8,128)(2,1)} %param.11, f32[256,32,512]{0,2,1:T(8,128)} %convolution_bitcast_fusion, bf16[256,32,512]{0,2,1:T(8,128)(2,1)} %copy.70), kind=kOutput, calls=%fused_computation.26 | convolution fusion | flops 2164260864 | bytes 37748736 | tf_op jit(solution)/shard_map/cef,ecd->fcd/dot_general | solution.py:49
  651.6 55.8 %all-to-all-done.2 = bf16[256,32,512]{2,1,0:T(8,128)(2,1)} async-done(((bf16[256,32,512]{2,1,0:T(8,128)(2,1)}), bf16[256,32,512]{2,1,0:T(8,128)(2,1)}, u32[]{:S(2)}, u32[]{:S(2)}) %all-to-all-start.2) | async-done | bytes 8388640 | tf_op jit(solution)/shard_map/all_to_all | solution.py:14
  707.3 8.3 copy.91
  715.6 14.5 %copy.92 = bf16[256,32,512]{2,1,0:T(8,128)(2,1)} copy(bf16[256,32,512]{0,2,1:T(8,128)(2,1)} %convert_bitcast_fusion.1) | data formatting | bytes 16777216 | tf_op jit(solution)/shard_map/optimization_barrier | solution.py:18
  730.1 36.5 %all-to-all-start.3 = ((bf16[256,32,512]{2,1,0:T(8,128)(2,1)}), bf16[256,32,512]{2,1,0:T(8,128)(2,1)}, u32[]{:S(2)}, u32[]{:S(2)}) async-start(bf16[256,32,512]{2,1,0:T(8,128)(2,1)} %copy.92), calls=%async_computation.3 | async-start | bytes 16777216 | tf_op jit(solution)/shard_map/all_to_all | solution.py:14
  766.7 14.9 %multiply_convert_fusion.1 = bf16[256,32,512]{0,2,1:T(8,128)(2,1)} fusion(f32[256,32,512]{0,2,1:T(8,128)} %convolution_bitcast_fusion.1, f32[256,32,512]{0,2,1:T(8,128)} %convolution_bitcast_fusion), kind=kLoop, calls=%fused_computation.14 | loop fusion | flops 8388608 | bytes 41943040 | tf_op jit(solution)/shard_map/convert_element_type | solution.py:54
  781.8 16.1 %fusion.9 = f32[16,512,512]{2,1,0:T(8,128)} fusion(bf16[16,512,512]{2,1,0:T(8,128)(2,1)} %bitcast.144, bf16[1,16,512,512]{3,2,1,0:T(8,128)(2,1)} %param.6), kind=kOutput, calls=%fused_computation.20 | convolution fusion | flops 4294967296 | bytes 33554432 | tf_op jit(solution)/shard_map/acd,abd->acb/dot_general | solution.py:67
  797.8 119.4 %all-to-all-done.3 = bf16[256,32,512]{2,1,0:T(8,128)(2,1)} async-done(((bf16[256,32,512]{2,1,0:T(8,128)(2,1)}), bf16[256,32,512]{2,1,0:T(8,128)(2,1)}, u32[]{:S(2)}, u32[]{:S(2)}) %all-to-all-start.3) | async-done | bytes 8388640 | tf_op jit(solution)/shard_map/all_to_all | solution.py:14
  917.3 8.3 copy.93
  925.5 15.7 %multiply_convert_fusion = bf16[16,512,512]{2,1,0:T(8,128)(2,1)} fusion(f32[16,512,512]{2,1,0:T(8,128)} %fusion.9, bf16[16,512,512]{2,1,0:T(8,128)(2,1)} %bitcast.146, bf16[16,512,512]{1,2,0:T(8,128)(2,1)} %fusion.2), kind=kOutput, calls=%fused_computation.13 | convolution fusion | flops 4307550208 | bytes 41943040 | tf_op jit(solution)/shard_map/fhd,fcd->fch/dot_general | solution.py:74
  941.3 2.2 copy.113
  943.5 3.0 copy.111
  946.6 11.4 %convert_bitcast_fusion = bf16[1,16,512,512]{2,3,1,0:T(8,128)(2,1)} fusion(bf16[16,512,512]{2,1,0:T(8,128)(2,1)} %bitcast.145, bf16[16,512,512]{2,1,0:T(8,128)(2,1)} %param.10), kind=kOutput, calls=%fused_computation.25 | convolution fusion | flops 4299161600 | bytes 25165824 | tf_op jit(solution)/shard_map/acb,acd->abd/dot_general | solution.py:64
  957.9 12.3 %copy.102 = bf16[1,16,512,512]{3,2,1,0:T(8,128)(2,1)} copy(bf16[1,16,512,512]{2,3,1,0:T(8,128)(2,1)} %convert_bitcast_fusion) | data formatting | bytes 16777216
  970.2 7.8 copy.104
  978.0 21.2 %fusion.8 = (bf16[1,16,512,512]{2,3,1,0:T(8,128)(2,1)}, bf16[1,16,512,512]{2,3,1,0:T(8,128)(2,1)}) fusion(bf16[1,16,512,512]{2,3,1,0:T(8,128)(2,1)} %copy.71, bf16[1,16,512,512]{2,3,1,0:T(8,128)(2,1)} %copy.69, bf16[16,512,512]{2,1,0:T(8,128)(2,1)} %bitcast.147, bf16[16,512,512]{2,1,0:T(8,128)(2,1)} %param.10), kind=kOutput, calls=%fused_computation.19 | convolution fusion | flops 4353687552 | bytes 50331648 | tf_op jit(solution)/shard_map/fch,fcd->fhd/dot_general | solution.py:68
  999.2 12.4 %copy.103 = bf16[1,16,512,512]{3,2,1,0:T(8,128)(2,1)} copy(bf16[1,16,512,512]{2,3,1,0:T(8,128)(2,1)} %get-tuple-element.42) | data formatting | bytes 16777216
  1011.6 12.3 %copy.101 = bf16[1,16,512,512]{3,2,1,0:T(8,128)(2,1)} copy(bf16[1,16,512,512]{2,3,1,0:T(8,128)(2,1)} %get-tuple-element.43) | data formatting | bytes 16777216
  1023.9 48.7 %reduce-scatter.8.cloned.1.call-done = bf16[16,512,256]{2,1,0:T(8,128)(2,1)} async-done(((bf16[16,512,512]{2,1,0:T(8,128)(2,1)}), bf16[16,512,256]{2,1,0:T(8,128)(2,1)}) %reduce-scatter.8.cloned.1.call-update) | async-done | bytes 4194320 | tf_op jit(solution)/shard_map/reduce_scatter | solution.py:76
  (45 shorter events, 26.5 us)
Async XLA Ops:
  115.4 15.3 %copy-start.6 = (bf16[1,16,32,512]{3,2,1,0:T(8,128)(2,1)S(1)}, bf16[1,16,32,512]{3,2,1,0:T(8,128)(2,1)}, u32[]{:S(2)}) copy-start(bf16[1,16,32,512]{3,2,1,0:T(8,128)(2,1)} %copy.80) | copy-start | bytes 1572868
  115.4 16.2 %copy-start.5 = (bf16[1,16,32,512]{3,2,1,0:T(8,128)(2,1)S(1)}, bf16[1,16,32,512]{3,2,1,0:T(8,128)(2,1)}, u32[]{:S(2)}) copy-start(bf16[1,16,32,512]{3,2,1,0:T(8,128)(2,1)} %copy.81) | copy-start | bytes 1572868
  115.4 17.0 %copy-start.4 = (bf16[1,16,32,512]{3,2,1,0:T(8,128)(2,1)S(1)}, bf16[1,16,32,512]{3,2,1,0:T(8,128)(2,1)}, u32[]{:S(2)}) copy-start(bf16[1,16,32,512]{3,2,1,0:T(8,128)(2,1)} %copy.82) | copy-start | bytes 1572868
  115.4 17.9 %copy-start.3 = (bf16[1,16,32,512]{3,2,1,0:T(8,128)(2,1)S(1)}, bf16[1,16,32,512]{3,2,1,0:T(8,128)(2,1)}, u32[]{:S(2)}) copy-start(bf16[1,16,32,512]{3,2,1,0:T(8,128)(2,1)} %copy.83) | copy-start | bytes 1572868
  115.4 18.7 %copy-start.2 = (bf16[1,16,32,512]{3,2,1,0:T(8,128)(2,1)S(1)}, bf16[1,16,32,512]{3,2,1,0:T(8,128)(2,1)}, u32[]{:S(2)}) copy-start(bf16[1,16,32,512]{3,2,1,0:T(8,128)(2,1)} %copy.84) | copy-start | bytes 1572868
  115.4 19.6 %copy-start.1 = (bf16[1,16,32,512]{3,2,1,0:T(8,128)(2,1)S(1)}, bf16[1,16,32,512]{3,2,1,0:T(8,128)(2,1)}, u32[]{:S(2)}) copy-start(bf16[1,16,32,512]{3,2,1,0:T(8,128)(2,1)} %copy.85) | copy-start | bytes 1572868
  137.5 158.2 %all-to-all-start = ((bf16[16,16,32,512]{3,2,1,0:T(8,128)(2,1)}), bf16[16,16,32,512]{3,2,1,0:T(8,128)(2,1)}, u32[]{:S(2)}, u32[]{:S(2)}) async-start(bf16[16,16,32,512]{3,2,1,0:T(8,128)(2,1)} %constant_dynamic-update-slice_fusion), calls=%async_computation | async-start | bytes 16777216 | tf_op jit(solution)/shard_map/all_to_all | solution.py:9
  295.7 16.0 %copy-start = (bf16[16,512,512]{2,1,0:T(8,128)(2,1)S(1)}, bf16[16,512,512]{2,1,0:T(8,128)(2,1)}, u32[]{:S(2)}) copy-start(bf16[16,512,512]{2,1,0:T(8,128)(2,1)} %fusion.19) | copy-start | bytes 25165828
  318.5 187.1 %all-to-all-start.1 = ((bf16[16,16,32,512]{3,2,1,0:T(8,128)(2,1)}), bf16[16,16,32,512]{3,2,1,0:T(8,128)(2,1)}, u32[]{:S(2)}, u32[]{:S(2)}) async-start(bf16[16,16,32,512]{3,2,1,0:T(8,128)(2,1)} %bitcast_dynamic-update-slice_fusion), calls=%async_computation.1 | async-start | bytes 16777216 | tf_op jit(solution)/shard_map/all_to_all | solution.py:9
  520.2 187.1 %all-to-all-start.2 = ((bf16[256,32,512]{2,1,0:T(8,128)(2,1)}), bf16[256,32,512]{2,1,0:T(8,128)(2,1)}, u32[]{:S(2)}, u32[]{:S(2)}) async-start(bf16[256,32,512]{2,1,0:T(8,128)(2,1)} %copy.90), calls=%async_computation.2 | async-start | bytes 16777216 | tf_op jit(solution)/shard_map/all_to_all | solution.py:14
  556.8 384.6 %reduce-scatter.10.cloned.1.call-start = ((), (), s32[]{:S(2)}) async-start(), calls=%async_computation.9 | async-start | bytes 6291456
  730.1 187.1 %all-to-all-start.3 = ((bf16[256,32,512]{2,1,0:T(8,128)(2,1)}), bf16[256,32,512]{2,1,0:T(8,128)(2,1)}, u32[]{:S(2)}, u32[]{:S(2)}) async-start(bf16[256,32,512]{2,1,0:T(8,128)(2,1)} %copy.92), calls=%async_computation.3 | async-start | bytes 16777216 | tf_op jit(solution)/shard_map/all_to_all | solution.py:14
  766.7 203.5 %reduce-scatter.6.cloned.1.call-start = ((), (), s32[]{:S(2)}) async-start(), calls=%async_computation.7 | async-start | bytes 12582912 | tf_op jit(solution)/shard_map/reduce_scatter | solution.py:62
  781.7 290.9 %reduce-scatter.8.cloned.1.call-start = ((), (), s32[]{:S(2)}) async-start(), calls=%async_computation.8 | async-start | bytes 12582912 | tf_op jit(solution)/shard_map/reduce_scatter | solution.py:76
Sparse Core Ops, SparseCore 0:
  637.2 55.6 reduce-scatter.9
  781.8 100.6 reduce-scatter.5
  941.4 131.1 reduce-scatter.7
